TPU v7x, 512 devices: a whole 4x8x8 slice. The times are simulated.
512 devices in a mesh: grp: 8 (over y_lo, core), own: 64 (over x, y_hi, z).
Axes of the slice: x: 4, y: 8 (y_hi: 2, y_lo: 4; y = y_hi * 4 + y_lo), z: 8, core: 2. Of those that a mesh axis runs over, the one named last changes fastest.
Arguments:
- activations: bfloat16 [65536, 1024], P(('grp', 'own'))
- out_grads: bfloat16 [65536, 1024], P(('grp', 'own')), may hold values from -0.01953125 to 0.01953125
- master: float32 [1024, 1024], P('own'), may hold values from -6 to 6
- moment: float32 [1024, 1024], P('own'), may hold values from 0.05 to 5
- left_root: bfloat16 [1024, 1024], P('own'), may hold values from -0.25 to 2.25, as said below
- right_root: bfloat16 [1024, 1024], P('own'), may hold values from -0.25 to 2.25, as said below
- stats_in: float32 [256, 16, 1024], P('own'), may hold values from -6 to 6
- tile_slot: int32 [128], replicated, may hold values from 0 to 255, as said below
Outputs:
- master_out: float32 [1024, 1024], P('own')
- moment_out: float32 [1024, 1024], P('own')
- stats_out: float32 [256, 16, 1024], P('own')
- weights: bfloat16 [1024, 1024], replicated
Inputs may be any that keep to these rules, and one draw needn't show every extreme that they name: `tile_slot`: distinct slot numbers; slot s belongs to owner s // 4; some owner holds 4 tiles. `left_root`: symmetric. `right_root`: symmetric.
All inputs are finite; a program needn't handle non-finite values.
Results may differ from a plain program's by a relative error of at most 0.005.
Values may be sent and summed in bfloat16 or wider, within the bound.
No kernel may reach another device: no remote copies, remote signals or barrier semaphores. Data moves between devices by JAX's collectives and lax.ppermute only.
A program may use at most 64 MiB of HBM per device.

v0:
```python
import jax
import jax.numpy as jnp
from jax import lax
from jax.sharding import PartitionSpec as P

stat_decay = 0.9
moment_decay = 0.95
learn_rate = 0.3
adam_eps = 1e-08
norm_eps = 1e-06


def local(activations, out_grads, master, moment, left_root, right_root, stats_in, tile_slot):
    owner_rows = master.shape[0]
    block_size = master.shape[1]
    capacity = stats_in.shape[0]
    tile_rows = stats_in.shape[1]
    tile_count = tile_slot.shape[0]
    owner_index = lax.axis_index("own")
    gradient = lax.psum(
        lax.dot_general(
            activations, out_grads, (((0,), (0,)), ((), ())), preferred_element_type=jnp.float32
        ),
        ("grp", "own"),
    )
    grad_rows = lax.dynamic_slice_in_dim(gradient, owner_index * owner_rows, owner_rows, 0)
    moment_out = moment_decay * moment + (1.0 - moment_decay) * grad_rows * grad_rows
    adam_dir = grad_rows / (jnp.sqrt(moment_out) + adam_eps)
    my_slots = owner_index * capacity + jnp.arange(capacity, dtype=jnp.int32)
    matches = (tile_slot[:, None] == my_slots[None, :]).astype(jnp.int32)
    tile_ids = jnp.sum(matches * jnp.arange(tile_count, dtype=jnp.int32)[:, None], axis=0)
    filled = jnp.sum(matches, axis=0)
    per_half = block_size // tile_rows

    def slot_update(packed):
        tile_id, slot_filled, old_tile = packed
        which_half = tile_id // per_half
        offset = (tile_id - which_half * per_half) * tile_rows

        def left_product():
            row_block = lax.dynamic_slice_in_dim(gradient, offset, tile_rows, 0)
            return lax.dot_general(
                row_block,
                gradient,
                (((1,), (1,)), ((), ())),
                precision=lax.Precision.HIGHEST,
                preferred_element_type=jnp.float32,
            )

        def right_product():
            column_block = lax.dynamic_slice_in_dim(gradient, offset, tile_rows, 1)
            return lax.dot_general(
                column_block,
                gradient,
                (((0,), (0,)), ((), ())),
                precision=lax.Precision.HIGHEST,
                preferred_element_type=jnp.float32,
            )

        product = lax.cond(which_half == 0, left_product, right_product)
        return jnp.where(
            slot_filled > 0, stat_decay * old_tile + (1.0 - stat_decay) / block_size * product, 0.0
        )

    stats_out = lax.map(slot_update, (tile_ids, filled, stats_in))
    grad_low = gradient.astype(jnp.bfloat16)
    left_mid = jnp.dot(left_root, grad_low, preferred_element_type=jnp.float32).astype(jnp.bfloat16)
    precond = jnp.dot(
        left_mid,
        lax.all_gather(right_root, "own", axis=0, tiled=True),
        preferred_element_type=jnp.float32,
    )
    adam_sum, precond_sum = lax.psum(
        (jnp.sum(adam_dir * adam_dir), jnp.sum(precond * precond)), "own"
    )
    graft_scale = jnp.sqrt(adam_sum) / (jnp.sqrt(precond_sum) + norm_eps)
    master_out = master - learn_rate * graft_scale * precond
    weights = lax.all_gather(master_out.astype(jnp.bfloat16), "own", axis=0, tiled=True)
    return (master_out, moment_out, stats_out, weights)


def solution(mesh):
    in_specs = (
        P(("grp", "own"), None),
        P(("grp", "own"), None),
        P("own", None),
        P("own", None),
        P("own", None),
        P("own", None),
        P("own", None, None),
        P(),
    )
    out_specs = (P("own", None), P("own", None), P("own", None, None), P())
    return jax.shard_map(local, mesh=mesh, in_specs=in_specs, out_specs=out_specs, check_vma=False)
```

profile of v0, /device:TPU:8, one launch (start us, length us, event | category | flops | bytes accessed | tf_op | source)
XLA Modules:
  0.0 686.9 jit_solution(6704430149430638157)
XLA Ops:
  8.0 0.0 copy-start
  8.0 0.0 copy-start.1
  8.0 0.0 copy-start.3
  8.0 0.0 all-reduce.3.cloned.1.call-start
  8.1 0.9 copy-done
  9.0 3.6 fusion.22
  12.6 0.0 all-reduce.3.cloned.1.call-update
  12.6 0.0 copy-start.2
  12.6 0.0 copy-start.4
  12.6 0.0 all-gather.3.cloned.1.call-start
  12.7 0.5 all-gather.3.cloned.1.call-update
  13.2 0.0 all-gather.5.cloned.1.call-start
  13.3 305.9 %all-reduce.3.cloned.1.call-done = f32[1024,1024]{1,0:T(8,128)} async-done(((f32[1024,1024]{1,0:T(8,128)}), f32[1024,1024]{1,0:T(8,128)}) %all-reduce.3.cloned.1.call-update) | async-done | bytes 4194320 | tf_op jit(solution)/shard_map/psum | solution.py:20
  319.2 0.0 copy-done.1
  319.2 2.1 multiply_reduce_fusion.1
  321.3 0.0 all-gather.3.cloned.1.call-done
  321.3 0.0 copy-done.3
  321.3 4.9 multiply_reduce_fusion
  326.2 221.8 %all-reduce = (f32[]{:T(128)}, f32[]{:T(128)}) all-reduce(f32[]{:T(128)} %get-tuple-element.119, f32[]{:T(128)} %get-tuple-element.121), channel_id=1, replica_groups=mesh['grp'=8,'own'=64] {'own'}, use_global_device_ids=true, to_apply=%region_2.0 | all-reduce | flops 2 | bytes 16 | tf_op jit(solution)/shard_map/psum | solution.py:73
  549.4 0.0 copy-done.2
  549.5 0.6 fusion.18
  550.1 0.0 all-gather.5.cloned.1.call-update
  550.2 0.0 copy-done.4
  550.2 0.2 fusion.17
  550.3 50.1 %while.12 = (s32[]{:T(128)}, f32[4,16,1024]{2,1,0:T(8,128)}, s32[4]{0:T(128)S(1)}, f32[4,16,1024]{2,1,0:T(8,128)}, s32[4]{0:T(128)S(1)}, /*index=5*/f32[1024,102...) while((s32[]{:T(128)}, f32[4,16,1024]{2,1,0:T(8,128)}, ...), condition=%wide.region_10.11_spmd, body=%wide.region_7.10_spmd.sunk | while | flops 201392144 | bytes 4982188 | solution.py:65
  550.4 0.7 dynamic_slice.42
  554.5 4.8 conditional.2
  554.5 4.8 fusion
  559.3 0.7 dynamic_slice.43
  560.6 1.5 bitcast_dynamic-update-slice_fusion.2
  562.1 0.7 dynamic_slice.42
  566.3 5.8 conditional.2
  566.3 5.8 fusion.3
  572.1 0.7 dynamic_slice.43
  573.4 1.5 bitcast_dynamic-update-slice_fusion.2
  574.9 0.7 dynamic_slice.42
  579.1 5.8 conditional.2
  579.1 5.8 fusion.3
  584.8 0.7 dynamic_slice.43
  586.2 1.5 bitcast_dynamic-update-slice_fusion.2
  587.7 0.7 dynamic_slice.42
  591.8 5.8 conditional.2
  591.9 5.8 fusion.3
  597.6 0.7 dynamic_slice.43
  599.0 1.5 bitcast_dynamic-update-slice_fusion.2
  600.5 75.9 %all-gather.5.cloned.1.call-done = bf16[1024,1024]{1,0:T(8,128)(2,1)} async-done(((bf16[16,1024]{1,0:T(8,128)(2,1)}), bf16[1024,1024]{1,0:T(8,128)(2,1)}) %all-gather.5.cloned.1.call-update) | async-done | bytes 2097168 | tf_op jit(solution)/shard_map/all_gather | solution.py:78
  676.4 3.1 copy.23
  (2 shorter events, 0.0 us)
Async XLA Ops:
  8.0 1.0 copy-start
  8.0 311.2 %copy-start.1 = (f32[16,1024]{1,0:T(8,128)S(1)}, f32[16,1024]{1,0:T(8,128)}, u32[]{:S(2)}) copy-start(f32[16,1024]{1,0:T(8,128)} %param.15) | copy-start | bytes 196612
  8.0 313.3 %copy-start.3 = (bf16[16,1024]{1,0:T(8,128)(2,1)S(1)}, bf16[16,1024]{1,0:T(8,128)(2,1)}, u32[]{:S(2)}) copy-start(bf16[16,1024]{1,0:T(8,128)(2,1)} %param.16) | copy-start | bytes 98308
  8.0 311.2 %all-reduce.3.cloned.1.call-start = ((), (), s32[]{:S(2)}) async-start(), calls=%async_computation | async-start | bytes 8388608 | tf_op jit(solution)/shard_map/psum | solution.py:20
  12.6 536.8 %copy-start.2 = (f32[16,1024]{1,0:T(8,128)S(1)}, f32[16,1024]{1,0:T(8,128)}, u32[]{:S(2)}) copy-start(f32[16,1024]{1,0:T(8,128)} %param.14) | copy-start | bytes 196612
  12.6 537.5 %copy-start.4 = (s32[128]{0:T(128)S(1)}, s32[128]{0:T(128)}, u32[]{:S(2)}) copy-start(s32[128]{0:T(128)} %param.19) | copy-start | bytes 1540
  12.6 308.7 %all-gather.3.cloned.1.call-start = ((), (), s32[]{:S(2)}) async-start(), calls=%async_computation.1 | async-start | bytes 2129920 | tf_op jit(solution)/shard_map/all_gather | solution.py:70
  13.2 663.2 %all-gather.5.cloned.1.call-start = ((), (), s32[]{:S(2)}) async-start(), calls=%async_computation.2 | async-start | bytes 2129920 | tf_op jit(solution)/shard_map/all_gather | solution.py:78
Sparse Core Ops, SparseCore 0:
  13.8 305.3 all-reduce.2
Sparse Core Ops, SparseCore 1:
  17.7 140.6 all-gather.2
  550.2 126.2 all-gather.4
where the time goes:
time: 688 us; the launch traced here: 687 us
  waiting for transfers between devices  382 us (56%)
  blocking collectives  222 us (32%)
  matrix products  30.6 us (4%)
  between operations  17 us (2%)
  loops' own time  16.8 us (2%)
  local copies, waits for them, and re-layouts  9.33 us (1%)
  other arithmetic  8.89 us (1%)
    psum x1, waiting for transfers between devices, local(): lax.psum(lax.dot_general(activations, out_grads, (((0,), (0,)), ((), ()))...  306 us
    psum x1, blocking collectives, local(): lax.psum((jnp.sum(adam_dir * adam_dir), jnp.sum(precond * precond)), 'own')  222 us
    all_gather x1, waiting for transfers between devices, local(): lax.all_gather(master_out.astype(jnp.bfloat16), 'own', axis=0, tiled=True)  75.9 us
    dot_general x3, matrix products, left_product(): lax.dot_general(row_block, gradient, (((1,), (1,)), ((), ())), precision=...  17.3 us
    another operation x1, loops' own time, local(): stats_out = lax.map(slot_update, (tile_ids, filled, stats_in))  16.7 us
  transfers between devices with their start and end apart: 3, of which 2 were waited for; matrix products, arithmetic and copies ran while one was open for 5% of the time, Pallas kernels for 0%

commit v1 on v0

--- a/solution.py
+++ b/solution.py
@@ -75,7 +75,12 @@
     )
     graft_scale = jnp.sqrt(adam_sum) / (jnp.sqrt(precond_sum) + norm_eps)
     master_out = master - learn_rate * graft_scale * precond
-    weights = lax.all_gather(master_out.astype(jnp.bfloat16), "own", axis=0, tiled=True)
+    weights = jnp.concatenate(
+        lax.all_to_all(
+            jnp.stack([master_out.astype(jnp.bfloat16)] * lax.axis_size("own")), "own", 0, 0
+        ),
+        axis=0,
+    )
     return (master_out, moment_out, stats_out, weights)
 
 

time: 688 us -> 622 us (0.904)
  the two profiles are of different devices: /device:TPU:8 before, /device:TPU:60 now
where the time goes in v1:
time: 622 us; the launch traced here: 621 us
  waiting for transfers between devices  307 us (49%)
  blocking collectives  185 us (30%)
  starting transfers between devices  49.4 us (8%)
  matrix products  31.6 us (5%)
  between operations  17 us (3%)
  loops' own time  13.6 us (2%)
  other arithmetic  8.88 us (1%)
  local copies, waits for them, and re-layouts  8.46 us (1%)
    psum x1, waiting for transfers between devices, local(): lax.psum(lax.dot_general(activations, out_grads, (((0,), (0,)), ((), ()))...  307 us
    psum x1, blocking collectives, local(): lax.psum((jnp.sum(adam_dir * adam_dir), jnp.sum(precond * precond)), 'own')  185 us
    all_to_all x1, starting transfers between devices, local(): lax.all_to_all(jnp.stack([master_out.astype(jnp.bfloat16)] * lax.axis_siz...  49.3 us
    dot_general x4, matrix products, left_product(): lax.dot_general(row_block, gradient, (((1,), (1,)), ((), ())), precision=...  23 us
    another operation x1, loops' own time, local(): stats_out = lax.map(slot_update, (tile_ids, filled, stats_in))  13.5 us
  transfers between devices with their start and end apart: 3, of which 1 were waited for; matrix products, arithmetic and copies ran while one was open for 6% of the time, Pallas kernels for 0%

profile of v1, /device:TPU:60, one launch (start us, length us, event | category | flops | bytes accessed | tf_op | source)
XLA Modules:
  0.0 621.0 jit_solution(14956953409244939951)
XLA Ops:
  8.0 0.0 copy-start
  8.0 0.0 copy-start.1
  8.0 0.0 copy-start.3
  8.0 0.0 all-reduce.3.cloned.1.call-start
  8.1 0.9 copy-done
  9.0 3.7 fusion.22
  12.6 0.0 all-reduce.3.cloned.1.call-update
  12.6 0.0 copy-start.2
  12.6 0.0 all-gather.2.cloned.1.call-start
  12.7 0.5 all-gather.2.cloned.1.call-update
  13.2 306.7 %all-reduce.3.cloned.1.call-done = f32[1024,1024]{1,0:T(8,128)} async-done(((f32[1024,1024]{1,0:T(8,128)}), f32[1024,1024]{1,0:T(8,128)}) %all-reduce.3.cloned.1.call-update) | async-done | bytes 4194320 | tf_op jit(solution)/shard_map/psum | solution.py:20
  319.9 0.0 copy-done.1
  320.0 2.1 multiply_reduce_fusion.1
  322.0 0.0 all-gather.2.cloned.1.call-done
  322.0 0.0 copy-done.3
  322.1 4.9 multiply_reduce_fusion
  327.0 0.0 copy-start.4
  327.0 184.7 %all-reduce = (f32[]{:T(128)}, f32[]{:T(128)}) all-reduce(f32[]{:T(128)} %get-tuple-element.119, f32[]{:T(128)} %get-tuple-element.121), channel_id=1, replica_groups=mesh['grp'=8,'own'=64] {'own'}, use_global_device_ids=true, to_apply=%region_2.0 | all-reduce | flops 2 | bytes 16 | tf_op jit(solution)/shard_map/psum | solution.py:73
  513.1 0.0 copy-done.2
  513.2 0.6 fusion.18
  513.8 1.6 stack.2
  515.4 49.3 %all-to-all-start = ((bf16[64,16,1024]{2,1,0:T(8,128)(2,1)}), bf16[64,16,1024]{2,1,0:T(8,128)(2,1)S(1)}, u32[]{:S(2)}, u32[]{:S(2)}) async-start(bf16[64,16,1024]{2,1,0:T(8,128)(2,1)} %stack.2), calls=%async_computation | async-start | bytes 4194304 | tf_op jit(solution)/shard_map/all_to_all | solution.py:79
  564.7 0.0 copy-done.4
  564.7 0.2 fusion.17
  564.9 47.3 %while.12 = (s32[]{:T(128)}, f32[4,16,1024]{2,1,0:T(8,128)}, s32[4]{0:T(128)S(1)}, f32[4,16,1024]{2,1,0:T(8,128)}, s32[4]{0:T(128)S(1)}, /*index=5*/f32[1024,102...) while((s32[]{:T(128)}, f32[4,16,1024]{2,1,0:T(8,128)}, ...), condition=%wide.region_10.11_spmd, body=%wide.region_7.10_spmd.sunk | while | flops 201392144 | bytes 4982188 | solution.py:65
  564.9 0.6 dynamic_slice.42
  568.3 5.8 conditional.2
  568.4 5.8 fusion.3
  574.1 0.6 dynamic_slice.43
  575.3 1.5 bitcast_dynamic-update-slice_fusion.2
  576.8 0.6 dynamic_slice.42
  580.1 5.8 conditional.2
  580.2 5.8 fusion.3
  585.9 0.6 dynamic_slice.43
  587.1 1.5 bitcast_dynamic-update-slice_fusion.2
  588.6 0.6 dynamic_slice.42
  592.0 5.8 conditional.2
  592.0 5.8 fusion.3
  597.7 0.6 dynamic_slice.43
  598.9 1.5 bitcast_dynamic-update-slice_fusion.2
  600.4 0.6 dynamic_slice.42
  603.8 5.8 conditional.2
  603.8 5.8 fusion.3
  609.6 0.6 dynamic_slice.43
  610.7 1.5 bitcast_dynamic-update-slice_fusion.2
  612.2 0.0 all-to-all-done
  612.2 1.3 copy.23
  (2 shorter events, 0.0 us)
Async XLA Ops:
  8.0 1.0 copy-start
  8.0 311.9 %copy-start.1 = (f32[16,1024]{1,0:T(8,128)S(1)}, f32[16,1024]{1,0:T(8,128)}, u32[]{:S(2)}) copy-start(f32[16,1024]{1,0:T(8,128)} %param.15) | copy-start | bytes 196612
  8.0 314.0 %copy-start.3 = (bf16[16,1024]{1,0:T(8,128)(2,1)S(1)}, bf16[16,1024]{1,0:T(8,128)(2,1)}, u32[]{:S(2)}) copy-start(bf16[16,1024]{1,0:T(8,128)(2,1)} %param.16) | copy-start | bytes 98308
  8.0 311.9 %all-reduce.3.cloned.1.call-start = ((), (), s32[]{:S(2)}) async-start(), calls=%async_computation.1 | async-start | bytes 8388608 | tf_op jit(solution)/shard_map/psum | solution.py:20
  12.6 500.5 %copy-start.2 = (f32[16,1024]{1,0:T(8,128)S(1)}, f32[16,1024]{1,0:T(8,128)}, u32[]{:S(2)}) copy-start(f32[16,1024]{1,0:T(8,128)} %param.14) | copy-start | bytes 196612
  12.6 309.4 %all-gather.2.cloned.1.call-start = ((), (), s32[]{:S(2)}) async-start(), calls=%async_computation.2 | async-start | bytes 2129920 | tf_op jit(solution)/shard_map/all_gather | solution.py:70
  327.0 237.8 %copy-start.4 = (s32[128]{0:T(128)S(1)}, s32[128]{0:T(128)}, u32[]{:S(2)}) copy-start(s32[128]{0:T(128)} %param.19) | copy-start | bytes 1540
  515.4 96.8 %all-to-all-start = ((bf16[64,16,1024]{2,1,0:T(8,128)(2,1)}), bf16[64,16,1024]{2,1,0:T(8,128)(2,1)S(1)}, u32[]{:S(2)}, u32[]{:S(2)}) async-start(bf16[64,16,1024]{2,1,0:T(8,128)(2,1)} %stack.2), calls=%async_computation | async-start | bytes 4194304 | tf_op jit(solution)/shard_map/all_to_all | solution.py:79
Sparse Core Ops, SparseCore 0:
  13.8 306.0 all-reduce.2
Sparse Core Ops, SparseCore 1:
  17.7 136.0 all-gather.1
